TPU v7x, 32 devices: a whole 2x2x4 slice. The times are simulated.
32 devices in a mesh: ctx: 4 (over y, core), row: 8 (over z, x).
Axes of the slice: x: 2, y: 2, z: 4, core: 2. Of those that a mesh axis runs over, the one named last changes fastest.
Arguments:
- queries: bfloat16 [16, 2, 4096], P('row'), may hold values from -400 to 400
- prefix_id: int32 [16], P('row'), may hold values from 0 to 7
- prefix_keys: bfloat16 [8, 1024, 512], P(None, ('ctx', 'row')), may hold values from -8 to 8
- prefix_values: bfloat16 [8, 1024, 512], P(None, ('ctx', 'row')), may hold values from -6 to 6
- pool_keys: bfloat16 [512, 64, 512], P(('ctx', 'row')), may hold values from -5 to 5
- pool_values: bfloat16 [512, 64, 512], P(('ctx', 'row')), may hold values from -6 to 6
- page_table: int32 [16, 32], P('row'), may hold values from 0 to 511, as said below
- suffix_len: int32 [16], P('row'), may hold values from 256 to 2048
- new_keys: bfloat16 [16, 2, 512], P('row'), may hold values from -6.25 to 6.25
- new_values: bfloat16 [16, 2, 512], P('row'), may hold values from -6 to 6
Outputs:
- attended: bfloat16 [16, 2, 4096], P('row')
Inputs may be any that keep to these rules, and one draw needn't show every extreme that they name: `page_table`: the 64 entries of the rows i with one value of i // 2 name different pool pages p with (p // 16) % (8) == i // 2, and together they name all such pages.
All inputs are finite; a program needn't handle non-finite values.
Results may differ from a plain program's by a relative error of at most 0.003.
Values may be sent and summed in bfloat16 or wider, within the bound.
No kernel may reach another device: no remote copies, remote signals or barrier semaphores. Data moves between devices by JAX's collectives and lax.ppermute only.
A program may use at most 64 MiB of HBM per device.

v0:
```python
import math
import jax
import jax.numpy as jnp
from jax import lax
from jax.sharding import PartitionSpec as P

H = 32
KVH = 4
HD = 128
MASKED_SCORE = -1e30


def joined(value, axis, join):
    pieces = jax.tree.map(lambda part: lax.all_gather(part, axis), value)
    head = jax.tree.map(lambda part: part[0], pieces)
    tail = jax.tree.map(lambda part: part[1:], pieces)
    running, _ = lax.scan(lambda running, share: (join(running, share), None), head, tail)
    return running


def combine_pair(earlier, later):
    highest = jnp.maximum(earlier[0], later[0])
    left_factor = jnp.exp(earlier[0] - highest)
    right_factor = jnp.exp(later[0] - highest)
    totals = left_factor * earlier[1] + right_factor * later[1]
    sums = left_factor[..., None] * earlier[2] + right_factor[..., None] * later[2]
    return (highest, totals, sums)


def fold_stack(stacked):
    peak_stack, total_stack, sum_stack = stacked
    highest = jnp.max(peak_stack, axis=0)
    factor = jnp.exp(peak_stack - highest[None])
    return (
        highest,
        jnp.sum(factor * total_stack, axis=0),
        jnp.sum(factor[..., None] * sum_stack, axis=0),
    )


def block_stats(scores, valid_mask, values, einsum_form):
    block_peak = jnp.max(jnp.where(valid_mask, scores, MASKED_SCORE), axis=-1)
    weights = jnp.where(valid_mask, jnp.exp(scores - block_peak[..., None]), 0.0).astype(
        jnp.bfloat16
    )
    block_total = jnp.sum(weights.astype(jnp.float32), axis=-1)
    block_sum = jnp.einsum(einsum_form, weights, values, preferred_element_type=jnp.float32)
    return (block_peak, block_total, block_sum)


def heads_merged(stats):
    lead = stats[0].shape[:2]
    return (
        stats[0].reshape(lead + (H,)),
        stats[1].reshape(lead + (H,)),
        stats[2].reshape(lead + (H, HD)),
    )


def per_device(
    queries,
    prefix_id,
    prefix_keys,
    prefix_values,
    pool_keys,
    pool_values,
    page_table,
    suffix_len,
    new_keys,
    new_values,
):
    rows_dev, step_count, feature_width = queries.shape
    groups = H // KVH
    score_scale = 1.0 / math.sqrt(HD)
    row_count = lax.axis_size("row")
    row_index = lax.axis_index("row")
    flat_index = lax.axis_index("ctx") * row_count + row_index
    own_query = queries.reshape(rows_dev, step_count, KVH, groups, HD)
    slot_count, page_len, kv_width = pool_keys.shape
    slot_ids = flat_index * slot_count + jnp.arange(slot_count, dtype=jnp.int32)
    slot_match = page_table[:, :, None] == slot_ids[None, None, :]
    entry_pos = jnp.arange(page_table.shape[1], dtype=jnp.int32)
    page_of = jnp.sum(jnp.where(slot_match, entry_pos[None, :, None], 0), axis=1)
    owned = jnp.any(slot_match, axis=1)
    token_pos = (
        page_of[:, :, None] * page_len + jnp.arange(page_len, dtype=jnp.int32)[None, None, :]
    )
    live_mask = owned[:, :, None] & (token_pos < suffix_len[:, None, None])
    live_mask = live_mask.reshape(rows_dev, 1, 1, 1, slot_count * page_len)
    flat_keys = pool_keys.reshape(slot_count * page_len, KVH, HD)
    flat_values = pool_values.reshape(slot_count * page_len, KVH, HD)
    suffix_scores = (
        jnp.einsum("rskgd,tkd->rskgt", own_query, flat_keys, preferred_element_type=jnp.float32)
        * score_scale
    )
    suffix_stats = block_stats(suffix_scores, live_mask, flat_values, "rskgt,tkd->rskgd")
    fresh_keys = new_keys.reshape(rows_dev, step_count, KVH, HD)
    fresh_values = new_values.reshape(rows_dev, step_count, KVH, HD)
    fresh_scores = (
        jnp.einsum("rskgd,rtkd->rskgt", own_query, fresh_keys, preferred_element_type=jnp.float32)
        * score_scale
    )
    causal = jnp.arange(step_count)[None, :] <= jnp.arange(step_count)[:, None]
    causal = causal.reshape(1, step_count, 1, 1, step_count)
    fresh_stats = heads_merged(block_stats(fresh_scores, causal, fresh_values, "rskgt,rtkd->rskgd"))
    every_query, every_prefix = (
        lax.all_gather(queries, "row", axis=0, tiled=True),
        lax.all_gather(prefix_id, "row", axis=0, tiled=True),
    )
    total_rows = every_query.shape[0]
    span_len = prefix_keys.shape[1]
    row_keys = jnp.take(prefix_keys, every_prefix, axis=0).reshape(total_rows, span_len, KVH, HD)
    row_values = jnp.take(prefix_values, every_prefix, axis=0).reshape(
        total_rows, span_len, KVH, HD
    )
    every_row = every_query.reshape(total_rows, step_count, KVH, groups, HD)
    prefix_scores = (
        jnp.einsum("rskgd,rtkd->rskgt", every_row, row_keys, preferred_element_type=jnp.float32)
        * score_scale
    )
    always = jnp.ones((1, 1, 1, 1, span_len), dtype=bool)
    prefix_stats = block_stats(prefix_scores, always, row_values, "rskgt,rtkd->rskgd")
    row_start = row_index * rows_dev
    own_prefix = tuple(
        (lax.dynamic_slice_in_dim(member, row_start, rows_dev, 0) for member in prefix_stats)
    )
    own_merged = combine_pair(own_prefix, suffix_stats)
    whole_stats = tuple(
        (
            lax.dynamic_update_slice_in_dim(whole_arr, piece_arr, row_start, 0)
            for whole_arr, piece_arr in zip(prefix_stats, own_merged)
        )
    )
    block_peak, block_total, block_sum = heads_merged(whole_stats)
    stacked = (
        lax.all_to_all(block_peak[None], "row", split_axis=1, concat_axis=0, tiled=True),
        lax.all_to_all(block_total[None], "row", split_axis=1, concat_axis=0, tiled=True),
        lax.all_to_all(block_sum[None], "row", split_axis=1, concat_axis=0, tiled=True),
    )
    local_stats = fold_stack(stacked)
    merged = joined(local_stats, "ctx", combine_pair)
    final_stats = combine_pair(merged, fresh_stats)
    result = (final_stats[2] / final_stats[1][..., None]).astype(jnp.bfloat16)
    return result.reshape(rows_dev, step_count, H * HD)


def solution(mesh):
    in_specs = (
        P("row", None, None),
        P("row"),
        P(None, ("ctx", "row"), None),
        P(None, ("ctx", "row"), None),
        P(("ctx", "row"), None, None),
        P(("ctx", "row"), None, None),
        P("row", None),
        P("row"),
        P("row", None, None),
        P("row", None, None),
    )
    out_specs = P("row", None, None)
    return jax.shard_map(
        per_device, mesh=mesh, in_specs=in_specs, out_specs=out_specs, check_vma=False
    )
```

profile of v0, /device:TPU:0, one launch (start us, length us, event | category | flops | bytes accessed | tf_op | source)
XLA Modules:
  0.0 102.8 jit_solution(12264209918332326410)
XLA Ops:
  0.0 0.9 compare_reduce_fusion
  0.9 0.9 fusion.21
  1.8 0.6 copy-done.11
  3.7 0.6 copy-done.10
  4.5 13.1 %all-reduce = s32[16]{0:T(128)S(1)} all-reduce(s32[16]{0:T(128)S(1)} %dynamic-update-slice), channel_id=1, replica_groups=mesh['ctx'=4,'row'=8] {'row'}, use_global_device_ids=true, to_apply=%add | all-reduce | flops 16 | bytes 128
  17.6 30.8 %all_gather.25 = bf16[16,2,4096]{2,1,0:T(2,128)(2,1)S(1)} all-gather(bf16[2,2,4096]{2,1,0:T(2,128)(2,1)S(1)} %copy-done.4), channel_id=1, replica_groups=mesh['ctx'=4,'row'=8] {'row'}, dimensions={0}, use_global_device_ids=true | all-gather | bytes 294912 | tf_op jit(solution)/shard_map/all_gather | solution.py:107
  52.3 0.9 copy-done.1
  53.5 0.6 copy-done.8
  54.8 0.9 convert_reduce_fusion
  55.8 0.7 reshape.185
  56.5 3.3 %all-to-all-start.1 = ((f32[8,1,128]{2,1,0:T(1,128)}), f32[8,1,128]{2,1,0:T(1,128)S(1)}, u32[]{:S(2)}, u32[]{:S(2)}) async-start(f32[8,1,128]{2,1,0:T(1,128)} %reshape.185), calls=%async_computation.1 | async-start | bytes 8192 | tf_op jit(solution)/shard_map/all_to_all | solution.py:137
  60.1 0.7 reshape.183
  61.1 5.2 %all-to-all-done.1 = f32[8,1,128]{2,1,0:T(1,128)S(1)} async-done(((f32[8,1,128]{2,1,0:T(1,128)}), f32[8,1,128]{2,1,0:T(1,128)S(1)}, u32[]{:S(2)}, u32[]{:S(2)}) %all-to-all-start.1) | async-done | bytes 4128 | tf_op jit(solution)/shard_map/all_to_all | solution.py:137
  66.3 3.3 %all-to-all-start = ((f32[8,1,128]{2,1,0:T(1,128)}), f32[8,1,128]{2,1,0:T(1,128)S(1)}, u32[]{:S(2)}, u32[]{:S(2)}) async-start(f32[8,1,128]{2,1,0:T(1,128)} %reshape.183), calls=%async_computation | async-start | bytes 8192 | tf_op jit(solution)/shard_map/all_to_all | solution.py:136
  69.6 1.2 %fusion.7 = f32[16,2,4,8,128]{4,3,1,2,0:T(8,128)S(1)} fusion(f32[16,2,4,8,128]{4,3,1,2,0:T(8,128)S(1)} %copy.183, s32[]{:T(128)S(6)} %select_n.36, bf16[1024,4,128,1,1]{2,1,0,4,3:T(4,128)(2,1)S(1)} %bitcast.92, bf16[2,2,4,8,1024]{4,3,1,0,2:T(8,128)(2,1)} %get-tuple-element.77, f32[16,4,128,2,8]{2,4,3,1,0:T(8,128)S(1)} %fusion.11, ...), kind=kOutput, calls=%fused_computation.18 | convolution fusion | flops 33603584 | bytes 1458180 | tf_op jit(solution)/shard_map/rskgt,tkd->rskgd/dot_general | solution.py:47
  70.8 0.9 copy.179
  71.7 4.4 %all-to-all-done = f32[8,1,128]{2,1,0:T(1,128)S(1)} async-done(((f32[8,1,128]{2,1,0:T(1,128)}), f32[8,1,128]{2,1,0:T(1,128)S(1)}, u32[]{:S(2)}, u32[]{:S(2)}) %all-to-all-start) | async-done | bytes 4128 | tf_op jit(solution)/shard_map/all_to_all | solution.py:136
  76.1 3.6 %all-to-all-start.2 = ((f32[1,16,2,32,128]{4,3,2,0,1:T(8,128)}), f32[1,16,2,32,128]{4,3,2,0,1:T(8,128)S(1)}, u32[]{:S(2)}, u32[]{:S(2)}) async-start(f32[1,16,2,32,128]{4,3,2,0,1:T(8,128)} %bitcast.84), calls=%async_computation.2 | async-start | bytes 1048576 | tf_op jit(solution)/shard_map/all_to_all | solution.py:138
  81.6 0.7 reduce.1
  82.4 0.7 reduce
  83.2 5.2 %all-gather.1 = f32[8,2,32]{2,1,0:T(2,128)S(1)} all-gather(f32[2,2,32]{2,1,0:T(2,128)S(1)} %copy.107), channel_id=3, replica_groups=mesh['ctx'=4,'row'=8] {'ctx'}, dimensions={0}, use_global_device_ids=true | all-gather | bytes 2560 | tf_op jit(solution)/shard_map/all_gather | solution.py:14
  89.0 5.1 %all-gather = f32[8,2,32]{2,1,0:T(2,128)S(1)} all-gather(f32[2,2,32]{2,1,0:T(2,128)S(1)} %copy.101), channel_id=2, replica_groups=mesh['ctx'=4,'row'=8] {'ctx'}, dimensions={0}, use_global_device_ids=true | all-gather | bytes 2560 | tf_op jit(solution)/shard_map/all_gather | solution.py:14
  95.0 5.8 %all-gather.2 = f32[8,2,32,128]{3,2,1,0:T(8,128)S(1)} all-gather(f32[2,2,32,128]{3,2,1,0:T(8,128)S(1)} %multiply_reduce_fusion), channel_id=4, replica_groups=mesh['ctx'=4,'row'=8] {'ctx'}, dimensions={0}, use_global_device_ids=true | all-gather | bytes 327680 | tf_op jit(solution)/shard_map/all_gather | solution.py:14
  100.8 0.7 slice-done
  (91 shorter events, 11.4 us)
Async XLA Ops:
  0.0 49.0 %copy-start = (bf16[8,32,512]{2,1,0:T(8,128)(2,1)S(1)}, bf16[8,32,512]{2,1,0:T(8,128)(2,1)}, u32[]{:S(2)}) copy-start(bf16[8,32,512]{2,1,0:T(8,128)(2,1)} %param.17) | copy-start | bytes 786436
  0.0 17.6 %copy-start.4 = (bf16[2,2,4096]{2,1,0:T(2,128)(2,1)S(1)}, bf16[2,2,4096]{2,1,0:T(2,128)(2,1)}, u32[]{:S(2)}) copy-start(bf16[2,2,4096]{2,1,0:T(2,128)(2,1)} %param.14) | copy-start | bytes 98308
  1.8 0.7 copy-start.11
  3.7 0.7 copy-start.10
  49.1 1.0 copy-start.3
  52.0 1.2 %copy-start.1 = (bf16[16,64,512]{2,1,0:T(8,128)(2,1)S(1)}, bf16[16,64,512]{2,1,0:T(8,128)(2,1)}, u32[]{:S(2)}) copy-start(bf16[16,64,512]{2,1,0:T(8,128)(2,1)} %param.18) | copy-start | bytes 3145732
  53.5 0.7 copy-start.8
  54.8 6.0 %copy-start.2 = (bf16[16,64,512]{2,1,0:T(8,128)(2,1)S(1)}, bf16[16,64,512]{2,1,0:T(8,128)(2,1)}, u32[]{:S(2)}) copy-start(bf16[16,64,512]{2,1,0:T(8,128)(2,1)} %param.19) | copy-start | bytes 3145732
  56.5 9.7 %all-to-all-start.1 = ((f32[8,1,128]{2,1,0:T(1,128)}), f32[8,1,128]{2,1,0:T(1,128)S(1)}, u32[]{:S(2)}, u32[]{:S(2)}) async-start(f32[8,1,128]{2,1,0:T(1,128)} %reshape.185), calls=%async_computation.1 | async-start | bytes 8192 | tf_op jit(solution)/shard_map/all_to_all | solution.py:137
  66.3 9.8 %all-to-all-start = ((f32[8,1,128]{2,1,0:T(1,128)}), f32[8,1,128]{2,1,0:T(1,128)S(1)}, u32[]{:S(2)}, u32[]{:S(2)}) async-start(f32[8,1,128]{2,1,0:T(1,128)} %reshape.183), calls=%async_computation | async-start | bytes 8192 | tf_op jit(solution)/shard_map/all_to_all | solution.py:136
  76.1 3.6 %copy-start.9 = (bf16[2,2,512]{2,1,0:T(2,128)(2,1)S(1)}, bf16[2,2,512]{2,1,0:T(2,128)(2,1)}, u32[]{:S(2)}) copy-start(bf16[2,2,512]{2,1,0:T(2,128)(2,1)} %param.22) | copy-start | bytes 12292
  76.1 18.7 %all-to-all-start.2 = ((f32[1,16,2,32,128]{4,3,2,0,1:T(8,128)}), f32[1,16,2,32,128]{4,3,2,0,1:T(8,128)S(1)}, u32[]{:S(2)}, u32[]{:S(2)}) async-start(f32[1,16,2,32,128]{4,3,2,0,1:T(8,128)} %bitcast.84), calls=%async_computation.2 | async-start | bytes 1048576 | tf_op jit(solution)/shard_map/all_to_all | solution.py:138
  80.2 0.7 copy-start.7
  88.4 0.6 copy-start.5
  94.1 0.6 copy-start.6
  100.8 0.7 slice-start
  100.8 0.7 slice-start.1
where the time goes:
time: 103 us
  blocking collectives  60 us (58%)
  local copies, waits for them, and re-layouts  13.1 us (13%)
  starting transfers between devices  10.3 us (10%)
  waiting for transfers between devices  9.62 us (9%)
  other arithmetic  5.62 us (5%)
  matrix products  3.1 us (3%)
    all_gather x1, blocking collectives, per_device(): lax.all_gather(queries, 'row', axis=0, tiled=True)  30.8 us
    all_gather x3, blocking collectives, joined(): pieces = jax.tree.map(lambda part: lax.all_gather(part, axis), value)  16.1 us
    unnamed x1, blocking collectives  13.1 us
    unnamed x32, local copies, waits for them, and re-layouts  7.34 us
    all_to_all x1, waiting for transfers between devices, per_device(): lax.all_to_all(block_total[None], 'row', split_axis=1, concat_axis=0, til...  5.21 us
    all_to_all x1, waiting for transfers between devices, per_device(): lax.all_to_all(block_peak[None], 'row', split_axis=1, concat_axis=0, tile...  4.41 us
    all_to_all x1, starting transfers between devices, per_device(): lax.all_to_all(block_sum[None], 'row', split_axis=1, concat_axis=0, tiled...  3.62 us
    all_to_all x1, starting transfers between devices, per_device(): lax.all_to_all(block_total[None], 'row', split_axis=1, concat_axis=0, til...  3.32 us
  transfers between devices with their start and end apart: 3, of which 2 were waited for; matrix products, arithmetic and copies ran while one was open for 6% of the time, Pallas kernels for 0%

commit v1 on v0

--- a/solution.py
+++ b/solution.py
@@ -135,7 +135,12 @@
     stacked = (
         lax.all_to_all(block_peak[None], "row", split_axis=1, concat_axis=0, tiled=True),
         lax.all_to_all(block_total[None], "row", split_axis=1, concat_axis=0, tiled=True),
-        lax.all_to_all(block_sum[None], "row", split_axis=1, concat_axis=0, tiled=True),
+        jnp.concatenate(
+            lax.all_to_all(
+                jnp.stack(jnp.split(block_sum[None], lax.axis_size("row"), axis=1)), "row", 0, 0
+            ),
+            axis=0,
+        ),
     )
     local_stats = fold_stack(stacked)
     merged = joined(local_stats, "ctx", combine_pair)

time: 103 us -> 107 us (1.039)
  local copies, waits for them, and re-layouts: 13.1 us -> 18 us
  waiting for transfers between devices: 9.62 us -> 6.02 us
  starting transfers between devices: 10.3 us -> 12.8 us
    all_to_all x1, waiting for transfers between devices: 5.21 us -> 0.01 us  [per_device(): lax.all_to_all(block_total[None], 'row', split_axis=1, concat_axis=0, til...]
    unnamed x32 -> x43, local copies, waits for them, and re-layouts: 7.34 us -> 11.7 us
    all_to_all x1, starting transfers between devices: 3.31 us -> 5.93 us  [per_device(): lax.all_to_all(block_peak[None], 'row', split_axis=1, concat_axis=0, tile...]
    all_to_all x1, waiting for transfers between devices: 4.41 us -> 6.01 us  [per_device(): lax.all_to_all(block_peak[None], 'row', split_axis=1, concat_axis=0, tile...]
  transfers between devices with their start and end apart: 3 -> 3, of which waited for: 2 -> 1; matrix products, arithmetic and copies ran while one was open for 6% -> 10% of each run, Pallas kernels for 0% -> 0%
where the time goes in v1:
time: 107 us
  blocking collectives  60 us (56%)
  local copies, waits for them, and re-layouts  18 us (17%)
  starting transfers between devices  12.8 us (12%)
  waiting for transfers between devices  6.02 us (6%)
  other arithmetic  5 us (5%)
  matrix products  3.74 us (3%)
    all_gather x1, blocking collectives, per_device(): lax.all_gather(queries, 'row', axis=0, tiled=True)  30.8 us
    all_gather x3, blocking collectives, joined(): pieces = jax.tree.map(lambda part: lax.all_gather(part, axis), value)  16.1 us
    unnamed x1, blocking collectives  13.1 us
    unnamed x43, local copies, waits for them, and re-layouts  11.7 us
    all_to_all x1, waiting for transfers between devices, per_device(): lax.all_to_all(block_peak[None], 'row', split_axis=1, concat_axis=0, tile...  6.01 us
    all_to_all x1, starting transfers between devices, per_device(): lax.all_to_all(block_peak[None], 'row', split_axis=1, concat_axis=0, tile...  5.93 us
    all_to_all x1, starting transfers between devices, per_device(): lax.all_to_all(jnp.stack(jnp.split(block_sum[None], lax.axis_size('row'),...  3.49 us
    all_to_all x1, starting transfers between devices, per_device(): lax.all_to_all(block_total[None], 'row', split_axis=1, concat_axis=0, til...  3.33 us
  transfers between devices with their start and end apart: 3, of which 1 were waited for; matrix products, arithmetic and copies ran while one was open for 10% of the time, Pallas kernels for 0%

profile of v1, /device:TPU:0, one launch (start us, length us, event | category | flops | bytes accessed | tf_op | source)
XLA Modules:
  0.0 106.5 jit_solution(10241464887252517934)
XLA Ops:
  0.0 0.9 compare_reduce_fusion
  0.9 0.9 fusion.30
  1.8 0.6 copy-done.13
  3.7 0.6 copy-done.12
  4.5 13.1 %all-reduce = s32[16]{0:T(128)S(1)} all-reduce(s32[16]{0:T(128)S(1)} %dynamic-update-slice), channel_id=1, replica_groups=mesh['ctx'=4,'row'=8] {'row'}, use_global_device_ids=true, to_apply=%add | all-reduce | flops 16 | bytes 128
  17.6 0.6 reshape.125
  18.3 30.8 %all_gather.25 = bf16[16,2,4096]{2,1,0:T(2,128)(2,1)S(1)} all-gather(bf16[2,2,4096]{2,1,0:T(2,128)(2,1)S(1)} %copy-done.5), channel_id=1, replica_groups=mesh['ctx'=4,'row'=8] {'row'}, dimensions={0}, use_global_device_ids=true | all-gather | bytes 294912 | tf_op jit(solution)/shard_map/all_gather | solution.py:107
  52.9 0.9 copy-done.1
  54.1 0.6 copy-done.10
  54.8 1.3 %select_reduce_fusion = (f32[2,2,4,8]{3,1,0,2:T(2,128)S(1)}, f32[2,2,4,8,1024]{4,3,1,0,2:T(8,128)S(1)}) fusion(pred[2,1024]{1,0:T(4,128)(4,1)S(1)} %compare_and_fusion, bf16[2,2,4,8,128]{4,3,2,1,0:T(8,128)(2,1)} %reshape.125, bf16[1024,4,128,1,1]{2,1,0,4,3:T(4,128)(2,1)S(1)} %bitcast.132), kind=kOutput, calls=%fused_computation.33 | convolution fusion | flops 33947520 | bytes 1608192 | tf_op jit(solution)/shard_map/rskgd,tkd->rskgt/dot_general | solution.py:93
  56.6 0.7 reshape.183
  57.3 3.3 %all-to-all-start.1 = ((f32[8,1,128]{2,1,0:T(1,128)}), f32[8,1,128]{2,1,0:T(1,128)S(1)}, u32[]{:S(2)}, u32[]{:S(2)}) async-start(f32[8,1,128]{2,1,0:T(1,128)} %reshape.183), calls=%async_computation.1 | async-start | bytes 8192 | tf_op jit(solution)/shard_map/all_to_all | solution.py:137
  61.0 1.1 %fusion.7 = f32[16,2,4,8,128]{4,3,1,2,0:T(8,128)S(1)} fusion(f32[16,2,4,8,128]{4,3,1,2,0:T(8,128)S(1)} %copy.188, s32[]{:T(128)S(6)} %select_n.36, bf16[1024,4,128,1,1]{2,1,0,4,3:T(4,128)(2,1)S(1)} %bitcast.133, bf16[2,2,4,8,1024]{4,3,1,0,2:T(8,128)(2,1)S(1)} %get-tuple-element.77, f32[16,4,128,2,8]{2,4,3,1,0:T(8,128)} %copy-done.4, ...), kind=kOutput, calls=%fused_computation.18 | convolution fusion | flops 33603584 | bytes 1458180 | tf_op jit(solution)/shard_map/rskgt,tkd->rskgd/dot_general | solution.py:47
  65.3 0.6 fusion.19
  66.7 0.7 reshape.181
  67.4 5.9 %all-to-all-start = ((f32[8,1,128]{2,1,0:T(1,128)}), f32[8,1,128]{2,1,0:T(1,128)S(1)}, u32[]{:S(2)}, u32[]{:S(2)}) async-start(f32[8,1,128]{2,1,0:T(1,128)} %reshape.181), calls=%async_computation | async-start | bytes 8192 | tf_op jit(solution)/shard_map/all_to_all | solution.py:136
  74.0 6.0 %all-to-all-done = f32[8,1,128]{2,1,0:T(1,128)S(1)} async-done(((f32[8,1,128]{2,1,0:T(1,128)}), f32[8,1,128]{2,1,0:T(1,128)S(1)}, u32[]{:S(2)}, u32[]{:S(2)}) %all-to-all-start) | async-done | bytes 4128 | tf_op jit(solution)/shard_map/all_to_all | solution.py:136
  80.0 3.5 %all-to-all-start.2 = ((f32[8,1,2,2,32,128]{5,4,3,2,1,0:T(8,128)}), f32[8,1,2,2,32,128]{5,4,3,2,1,0:T(8,128)S(1)}, u32[]{:S(2)}, u32[]{:S(2)}) async-start(f32[8,1,2,2,32,128]{5,4,3,2,1,0:T(8,128)} %fusion.17), calls=%async_computation.2 | async-start | bytes 1048576 | tf_op jit(solution)/shard_map/all_to_all | solution.py:139
  85.4 0.7 reduce.1
  86.2 0.7 reduce
  87.0 5.2 %all-gather.1 = f32[8,2,32]{2,1,0:T(2,128)S(1)} all-gather(f32[2,2,32]{2,1,0:T(2,128)S(1)} %copy.113), channel_id=3, replica_groups=mesh['ctx'=4,'row'=8] {'ctx'}, dimensions={0}, use_global_device_ids=true | all-gather | bytes 2560 | tf_op jit(solution)/shard_map/all_gather | solution.py:14
  92.8 5.1 %all-gather = f32[8,2,32]{2,1,0:T(2,128)S(1)} all-gather(f32[2,2,32]{2,1,0:T(2,128)S(1)} %copy.107), channel_id=2, replica_groups=mesh['ctx'=4,'row'=8] {'ctx'}, dimensions={0}, use_global_device_ids=true | all-gather | bytes 2560 | tf_op jit(solution)/shard_map/all_gather | solution.py:14
  98.7 5.8 %all-gather.2 = f32[8,2,32,128]{3,2,1,0:T(8,128)S(1)} all-gather(f32[2,2,32,128]{3,2,1,0:T(8,128)S(1)} %fusion.11), channel_id=4, replica_groups=mesh['ctx'=4,'row'=8] {'ctx'}, dimensions={0}, use_global_device_ids=true | all-gather | bytes 327680 | tf_op jit(solution)/shard_map/all_gather | solution.py:14
  104.6 0.7 slice-done
  (103 shorter events, 15.5 us)
Async XLA Ops:
  0.0 49.6 %copy-start = (bf16[8,32,512]{2,1,0:T(8,128)(2,1)S(1)}, bf16[8,32,512]{2,1,0:T(8,128)(2,1)}, u32[]{:S(2)}) copy-start(bf16[8,32,512]{2,1,0:T(8,128)(2,1)} %param.17) | copy-start | bytes 786436
  0.0 17.6 %copy-start.5 = (bf16[2,2,4096]{2,1,0:T(2,128)(2,1)S(1)}, bf16[2,2,4096]{2,1,0:T(2,128)(2,1)}, u32[]{:S(2)}) copy-start(bf16[2,2,4096]{2,1,0:T(2,128)(2,1)} %param.14) | copy-start | bytes 98308
  1.8 0.7 copy-start.13
  3.7 0.7 copy-start.12
  49.7 1.0 copy-start.3
  52.6 1.2 %copy-start.1 = (bf16[16,64,512]{2,1,0:T(8,128)(2,1)S(1)}, bf16[16,64,512]{2,1,0:T(8,128)(2,1)}, u32[]{:S(2)}) copy-start(bf16[16,64,512]{2,1,0:T(8,128)(2,1)} %param.18) | copy-start | bytes 3145732
  53.8 6.8 %copy-start.4 = (f32[16,4,128,2,8]{2,4,3,1,0:T(8,128)}, f32[16,4,128,2,8]{2,4,3,1,0:T(8,128)S(1)}, u32[]{:S(2)}) copy-start(f32[16,4,128,2,8]{2,4,3,1,0:T(8,128)S(1)} %fusion.12) | copy-start | bytes 1572868
  54.1 0.7 copy-start.10
  56.1 4.6 %copy-start.2 = (bf16[16,64,512]{2,1,0:T(8,128)(2,1)S(1)}, bf16[16,64,512]{2,1,0:T(8,128)(2,1)}, u32[]{:S(2)}) copy-start(bf16[16,64,512]{2,1,0:T(8,128)(2,1)} %param.19) | copy-start | bytes 3145732
  57.3 10.1 %all-to-all-start.1 = ((f32[8,1,128]{2,1,0:T(1,128)}), f32[8,1,128]{2,1,0:T(1,128)S(1)}, u32[]{:S(2)}, u32[]{:S(2)}) async-start(f32[8,1,128]{2,1,0:T(1,128)} %reshape.183), calls=%async_computation.1 | async-start | bytes 8192 | tf_op jit(solution)/shard_map/all_to_all | solution.py:137
  67.4 12.6 %all-to-all-start = ((f32[8,1,128]{2,1,0:T(1,128)}), f32[8,1,128]{2,1,0:T(1,128)S(1)}, u32[]{:S(2)}, u32[]{:S(2)}) async-start(f32[8,1,128]{2,1,0:T(1,128)} %reshape.181), calls=%async_computation | async-start | bytes 8192 | tf_op jit(solution)/shard_map/all_to_all | solution.py:136
  74.0 9.5 %copy-start.8 = (bf16[2,2,4,8,128]{4,3,2,1,0:T(8,128)(2,1)S(1)}, bf16[2,2,4,8,128]{4,3,2,1,0:T(8,128)(2,1)}, u32[]{:S(2)}) copy-start(bf16[2,2,4,8,128]{4,3,2,1,0:T(8,128)(2,1)} %reshape.125) | copy-start | bytes 98308
  74.0 9.5 %copy-start.11 = (bf16[2,2,512]{2,1,0:T(2,128)(2,1)S(1)}, bf16[2,2,512]{2,1,0:T(2,128)(2,1)}, u32[]{:S(2)}) copy-start(bf16[2,2,512]{2,1,0:T(2,128)(2,1)} %param.22) | copy-start | bytes 12292
  80.0 18.5 %all-to-all-start.2 = ((f32[8,1,2,2,32,128]{5,4,3,2,1,0:T(8,128)}), f32[8,1,2,2,32,128]{5,4,3,2,1,0:T(8,128)S(1)}, u32[]{:S(2)}, u32[]{:S(2)}) async-start(f32[8,1,2,2,32,128]{5,4,3,2,1,0:T(8,128)} %fusion.17), calls=%async_computation.2 | async-start | bytes 1048576 | tf_op jit(solution)/shard_map/all_to_all | solution.py:139
  84.0 0.7 copy-start.9
  92.2 0.6 copy-start.6
  97.9 0.6 copy-start.7
  104.6 0.7 slice-start
  104.6 0.7 slice-start.1
